TPU v7x, 512 devices: a whole 4x4x16 slice. The times are simulated.
512 devices in a mesh: dp: 4 (over z_hi, core), tm: 8 (over z_lo), height: 16 (over x, y).
Axes of the slice: x: 4, y: 4, z: 16 (z_hi: 2, z_lo: 8; z = z_hi * 8 + z_lo), core: 2. Of those that a mesh axis runs over, the one named last changes fastest.
Arguments:
- clips: bfloat16 [4, 16, 64, 128, 128], P('dp', 'tm', 'height'), may hold values from -6 to 6
- frame_counts: int32 [4, 5], P('dp'), may hold values from 1 to 9, 16 in all within a row
- conv_first: bfloat16 [3, 3, 3, 128, 128], replicated, may hold values from -0.109375 to 0.109375
- conv_down: bfloat16 [3, 3, 3, 128, 128], replicated, may hold values from -0.109375 to 0.109375
- out_cotangent: bfloat16 [4, 8, 32, 64, 128], P('dp', 'tm', 'height'), may hold values from -6 to 6
Outputs:
- encoded: bfloat16 [4, 8, 32, 64, 128], P('dp', 'tm', 'height')
- grad_first: bfloat16 [3, 3, 3, 128, 128], P(None, None, None, 'dp')
- grad_down: bfloat16 [3, 3, 3, 128, 128], P(None, None, None, 'dp')
Inputs may be any that keep to these rules, and one draw needn't show every extreme that they name: `frame_counts`: each sequence's 5 clip lengths sum to 16; in every sequence one clip has exactly 9 frames.
All inputs are finite; a program needn't handle non-finite values.
Results may differ from a plain program's by a relative error of at most 0.0059.
Values may be sent and summed in bfloat16 or wider, within the bound.
No kernel may reach another device: no remote copies, remote signals or barrier semaphores. Data moves between devices by JAX's collectives and lax.ppermute only.
A program may use at most 64 MiB of HBM per device.

v0:
```python
import math
import jax
import jax.numpy as jnp
from jax import lax
from jax.sharding import PartitionSpec as P


def padded_2(cells, sides, width):
    for axis, dim in sides:
        count = lax.axis_size(axis)
        ends = count - 1
        head = lax.slice_in_dim(cells, 0, width, axis=dim)
        tail = lax.slice_in_dim(cells, cells.shape[dim] - width, cells.shape[dim], axis=dim)
        cells = jnp.concatenate(
            [
                lax.ppermute(tail, axis, [(i, (i + 1) % count) for i in range(ends)]),
                cells,
                lax.ppermute(head, axis, [((i + 1) % count, i) for i in range(ends)]),
            ],
            axis=dim,
        )
    return cells


def shifted(value, axis, steps):
    count = lax.axis_size(axis)
    leading, last = (max(0, -steps), min(count, count - steps))
    return lax.ppermute(value, axis, [(source, source + steps) for source in range(leading, last)])


def unfold(frame_slab, stride, pad_cols):
    padded = jnp.pad(frame_slab, ((0, 0), (0, 0), pad_cols, (0, 0)))
    out_rows = (padded.shape[1] - 3) // stride + 1
    out_cols = (padded.shape[2] - 3) // stride + 1
    pieces = []
    for tap_row in range(3):
        for tap_col in range(3):
            pieces.append(
                padded[
                    :,
                    tap_row : tap_row + stride * (out_rows - 1) + 1 : stride,
                    tap_col : tap_col + stride * (out_cols - 1) + 1 : stride,
                ]
            )
    joined = jnp.concatenate(pieces, axis=-1)
    return (joined.reshape(-1, joined.shape[-1]), (frame_slab.shape[0], out_rows, out_cols))


def conv_layer(extended, weight, tap_mask, out_frames, stride, pad_cols):
    channels_out = weight.shape[-1]
    summed = None
    for tap_time in range(3):
        frame_slab = extended[tap_time : tap_time + stride * (out_frames - 1) + 1 : stride]
        columns, shape_out = unfold(frame_slab, stride, pad_cols)
        kernel = weight[tap_time].reshape(-1, channels_out)
        tap_term = jnp.dot(columns, kernel, preferred_element_type=jnp.float32).reshape(
            shape_out + (channels_out,)
        )
        tap_term = tap_term * tap_mask[:, tap_time][:, None, None, None]
        summed = tap_term if summed is None else summed + tap_term
    return summed


def weight_grad(extended, grads, tap_mask, stride, pad_cols):
    out_frames = grads.shape[0]
    blocks = []
    for tap_time in range(3):
        frame_slab = extended[tap_time : tap_time + stride * (out_frames - 1) + 1 : stride]
        columns, shape_out = unfold(frame_slab, stride, pad_cols)
        masked = grads * tap_mask[:, tap_time].astype(jnp.bfloat16)[:, None, None, None]
        blocks.append(
            jnp.dot(
                columns.T, masked.reshape(-1, grads.shape[-1]), preferred_element_type=jnp.float32
            )
        )
    stacked = jnp.stack(blocks)
    return stacked.reshape(3, 3, 3, extended.shape[-1], grads.shape[-1])


def hidden_grad(grads_ext, weight, mask_ext):
    pieces = []
    for tap_time in range(3):
        masked = grads_ext * mask_ext[:, tap_time].astype(jnp.bfloat16)[:, None, None, None]
        kernel = jnp.transpose(weight[tap_time][::-1, ::-1], (0, 1, 3, 2))
        spread = lax.conv_general_dilated(
            masked,
            kernel,
            (1, 1),
            ((2, 0), (2, 2)),
            lhs_dilation=(2, 2),
            dimension_numbers=("NHWC", "HWIO", "NHWC"),
            preferred_element_type=jnp.float32,
        )
        pieces.append(spread[:, 1:, 1:])
    even_frames = pieces[2][:-1] + pieces[0][1:]
    odd_frames = pieces[1][1:]
    merged = jnp.stack([even_frames, odd_frames], axis=1)
    return merged.reshape((2 * even_frames.shape[0],) + even_frames.shape[1:])


def positions(counts_row, frame_index):
    starts = jnp.cumsum(counts_row) - counts_row
    latest = jnp.max(jnp.where(starts[None, :] <= frame_index[:, None], starts[None, :], 0), axis=1)
    return frame_index - latest


def tap_masks(place):
    return (place[:, None] >= (2 - jnp.arange(3, dtype=jnp.int32))[None, :]).astype(jnp.float32)


def body(clips, frame_counts, conv_first, conv_down, out_cotangent):
    frames_dev = clips.shape[1]
    rows_dev = clips.shape[2]
    columns_all = clips.shape[3]
    down_frames = frames_dev // 2
    counts_row = frame_counts[0]
    first_frame = lax.axis_index("tm") * frames_dev
    frame_index = first_frame + jnp.arange(frames_dev, dtype=jnp.int32)
    first_mask = tap_masks(positions(counts_row, frame_index))
    down_index = first_frame + 2 * jnp.arange(down_frames + 1, dtype=jnp.int32)
    mask_ext = tap_masks(positions(counts_row, down_index))
    down_mask = mask_ext[:down_frames]
    with_rows = padded_2(clips[0], (("height", 1),), 1)
    earlier = shifted(with_rows, "tm", 1)
    input_ext = jnp.concatenate([earlier, with_rows], axis=0)
    pre_act = conv_layer(input_ext, conv_first, first_mask, frames_dev, 1, (1, 1))
    hidden = jax.nn.silu(pre_act).astype(jnp.bfloat16)
    above = shifted(hidden[:, rows_dev - 1 :], "height", 1)
    hidden_rows = jnp.concatenate([above, hidden], axis=1)
    hidden_past = shifted(hidden_rows, "tm", 1)
    hidden_ext = jnp.concatenate([hidden_past, hidden_rows], axis=0)
    encoded = conv_layer(hidden_ext, conv_down, down_mask, down_frames, 2, (1, 0)).astype(
        jnp.bfloat16
    )
    cells_all = (
        lax.axis_size("dp")
        * clips.shape[0]
        * down_frames
        * lax.axis_size("tm")
        * (rows_dev // 2)
        * lax.axis_size("height")
        * (columns_all // 2)
    )
    scale = 1.0 / math.sqrt(cells_all)
    grads = (out_cotangent[0].astype(jnp.float32) * scale).astype(jnp.bfloat16)
    down_local = weight_grad(hidden_ext, grads, down_mask, 2, (1, 0))
    below = shifted(grads[:, 0:1], "height", -1)
    grads_rows = jnp.concatenate([grads, below], axis=1)
    grads_next = shifted(grads_rows, "tm", -1)
    grads_ext = jnp.concatenate([grads_rows, grads_next], axis=0)
    back_hidden = hidden_grad(grads_ext, conv_down, mask_ext).astype(jnp.bfloat16)
    sigma = jax.nn.sigmoid(pre_act)
    pre_grad = (back_hidden.astype(jnp.float32) * sigma * (1.0 + pre_act * (1.0 - sigma))).astype(
        jnp.bfloat16
    )
    first_local = weight_grad(input_ext, pre_grad, first_mask, 1, (1, 1))
    share = conv_first.shape[3] // lax.axis_size("dp")
    summed_first, summed_down = lax.psum((first_local, down_local), ("dp", "tm", "height"))
    offset = lax.axis_index("dp") * share
    summed_first = lax.dynamic_slice_in_dim(summed_first, offset, share, 3)
    summed_down = lax.dynamic_slice_in_dim(summed_down, offset, share, 3)
    return (encoded[None], summed_first.astype(jnp.bfloat16), summed_down.astype(jnp.bfloat16))


def solution(mesh):
    in_specs = (
        P("dp", "tm", "height", None, None),
        P("dp", None),
        P(),
        P(),
        P("dp", "tm", "height", None, None),
    )
    out_specs = (
        P("dp", "tm", "height", None, None),
        P(None, None, None, "dp", None),
        P(None, None, None, "dp", None),
    )
    return jax.shard_map(body, mesh=mesh, in_specs=in_specs, out_specs=out_specs, check_vma=False)
```

profile of v0, /device:TPU:32, one launch (start us, length us, event | category | flops | bytes accessed | tf_op | source)
XLA Modules:
  0.0 263.5 jit_solution(3750914941561490961)
XLA Ops:
  0.6 1.0 fusion.93
  1.6 3.5 %collective-permute-start = (bf16[2,1,128,128]{3,2,1,0:T(8,128)(2,1)S(1)}, bf16[2,1,128,128]{3,2,1,0:T(8,128)(2,1)S(1)}, u32[]{:S(2)}, u32[]{:S(2)}) collective-permute-start(bf16[2,1,128,128]{3,2,1,0:T(8,128)(2,1)S(1)} %get-tuple-element.17), channel_id=1, source_target_pairs={{0,1},{1,2},{2,3},{3,4},{4,5},{5,6},{6,7},{7,8},{8,9},{9,10},{10,1... | collective-permute-start | bytes 196616 | tf_op jit(solution)/shard_map/ppermute | solution.py:16
  5.1 1.3 collective-permute-start.1
  6.4 0.8 fusion.63
  7.2 1.3 collective-permute-start.5
  8.5 0.8 reduce-window_clone.1
  9.4 0.7 subtract_bitcast_fusion
  10.0 0.2 fusion.68
  10.4 1.2 fusion.91
  11.6 0.9 fusion.90
  12.5 0.5 fusion.94
  13.1 0.6 slice.447
  13.7 0.6 slice.451
  16.0 5.2 %collective-permute-start.6 = (bf16[1,3,64,128]{3,2,1,0:T(8,128)(2,1)S(1)}, bf16[1,3,64,128]{3,2,1,0:T(8,128)(2,1)S(1)}, u32[]{:S(2)}, u32[]{:S(2)}) collective-permute-start(bf16[1,3,64,128]{3,2,1,0:T(8,128)(2,1)S(1)} %pad_maximum_fusion.7), channel_id=1, source_target_pairs={{16,0},{32,16},{48,32},{64,48},{80,64},{96,80},{112,96},{17,1},{33... | collective-permute-start | bytes 147464 | tf_op jit(solution)/shard_map/ppermute | solution.py:28
  21.3 1.9 collective-permute-start.2
  23.4 1.3 multiply_bitcast_fusion.1
  25.1 0.3 convolution_select_fusion.2
  25.4 0.3 fusion.4
  25.8 0.1 slice_dynamic-update-slice_fusion.10
  25.9 0.1 slice_dynamic-update-slice_fusion.9
  26.1 0.3 fusion.3
  26.5 0.1 slice_dynamic-update-slice_fusion.8
  26.9 0.1 slice_dynamic-update-slice_fusion.7
  27.1 0.1 slice_dynamic-update-slice_fusion.6
  27.2 3.8 %collective-permute-done.2 = bf16[2,6,128,128]{3,2,1,0:T(8,128)(2,1)S(1)} collective-permute-done((bf16[2,6,128,128]{3,2,1,0:T(8,128)(2,1)S(1)}, bf16[2,6,128,128]{3,2,1,0:T(8,128)(2,1)S(1)}, u32[]{:S(2)}, u32[]{:S(2)}) %collective-permute-start.2) | collective-permute-done | bytes 393248 | tf_op jit(solution)/shard_map/ppermute | solution.py:28
  31.3 0.1 slice_dynamic-update-slice_fusion.16
  31.4 0.1 slice_dynamic-update-slice_fusion.15
  31.6 0.1 slice_dynamic-update-slice_fusion.14
  31.7 0.1 slice_dynamic-update-slice_fusion.13
  31.9 0.1 slice_dynamic-update-slice_fusion.12
  32.0 0.8 convolution_multiply_fusion.1
  33.0 0.1 slice_dynamic-update-slice_fusion.22
  33.1 0.1 slice_dynamic-update-slice_fusion.21
  33.3 0.1 slice_dynamic-update-slice_fusion.20
  33.4 0.1 slice_dynamic-update-slice_fusion.19
  33.7 0.8 fusion.1
  34.5 0.9 fusion.10
  35.5 5.2 %collective-permute-start.3 = (bf16[2,1,128,128]{3,2,1,0:T(8,128)(2,1)S(1)}, bf16[2,1,128,128]{3,2,1,0:T(8,128)(2,1)S(1)}, u32[]{:S(2)}, u32[]{:S(2)}) collective-permute-start(bf16[2,1,128,128]{3,2,1,0:T(8,128)(2,1)S(1)} %slice.437), channel_id=1, source_target_pairs={{0,1},{1,2},{2,3},{3,4},{4,5},{5,6},{6,7},{7,8},{8,9},{9,10},{10,1... | collective-permute-start | bytes 196616 | tf_op jit(solution)/shard_map/ppermute | solution.py:28
  40.7 0.9 fusion.26
  41.5 0.9 fusion.24
  42.4 0.9 fusion.22
  43.3 0.2 pad_maximum_fusion
  44.2 0.1 slice.408
  44.4 0.1 slice.409
  44.5 0.2 slice.410
  44.8 3.2 %collective-permute-start.4 = (bf16[2,5,128,128]{3,2,1,0:T(8,128)(2,1)S(1)}, bf16[2,5,128,128]{3,2,1,0:T(8,128)(2,1)S(1)}, u32[]{:S(2)}, u32[]{:S(2)}) collective-permute-start(bf16[2,5,128,128]{3,2,1,0:T(8,128)(2,1)S(1)} %pad_maximum_fusion.2), channel_id=1, source_target_pairs={{0,16},{16,32},{32,48},{48,64},{64,80},{80,96},{96,112},{1,17},{17... | collective-permute-start | bytes 983048 | tf_op jit(solution)/shard_map/ppermute | solution.py:28
  48.3 1.1 convolution_bitcast_fusion
  49.4 4.4 %collective-permute-done.4 = bf16[2,5,128,128]{3,2,1,0:T(8,128)(2,1)S(1)} collective-permute-done((bf16[2,5,128,128]{3,2,1,0:T(8,128)(2,1)S(1)}, bf16[2,5,128,128]{3,2,1,0:T(8,128)(2,1)S(1)}, u32[]{:S(2)}, u32[]{:S(2)}) %collective-permute-start.4) | collective-permute-done | bytes 327712 | tf_op jit(solution)/shard_map/ppermute | solution.py:28
  54.5 0.1 slice.396
  54.7 0.1 slice.397
  54.8 0.2 slice.398
  55.8 0.1 slice.384
  55.9 0.1 slice.385
  56.1 0.2 slice.386
  56.9 0.3 convolution_bitcast_fusion.1
  57.2 0.3 copy-done.4
  57.5 0.3 convolution_bitcast_fusion.2
  57.8 1.2 pad_maximum_fusion.1
  58.9 196.0 %all-reduce.8 = (bf16[3,3,3,128,128]{4,3,2,1,0:T(8,128)(2,1)}, bf16[3,3,3,128,128]{4,3,2,1,0:T(8,128)(2,1)}) all-reduce(f32[3,3,3,128,128]{4,3,2,1,0:T(8,128)S(1)} %pad_maximum_fusion, f32[3,3,3,128,128]{4,3,2,1,0:T(8,128)S(1)} %pad_maximum_fusion.1), channel_id=1, replica_groups=mesh['dp'=4,'tm'=8,'height'=16] {'dp','tm','height'}, use_global_device_ids=true, to_apply=%region_3.4 | all-reduce | flops 884736 | bytes 5308416 | tf_op jit(solution)/shard_map/psum | solution.py:158
  255.0 1.7 dynamic-slice_convert_fusion
  256.7 1.6 dynamic-slice_convert_fusion.1
  258.3 1.8 convolution_multiply_fusion.5
  260.1 1.9 fusion.6
  262.1 1.4 fusion.8
  (122 shorter events, 4.5 us)
Async XLA Ops:
  0.6 20.6 %copy-start = (bf16[1,2,4,128,128]{4,3,2,1,0:T(8,128)(2,1)S(1)}, bf16[1,2,4,128,128]{4,3,2,1,0:T(8,128)(2,1)}, u32[]{:S(2)}) copy-start(bf16[1,2,4,128,128]{4,3,2,1,0:T(8,128)(2,1)} %param.5) | copy-start | bytes 786436
  0.6 10.9 %copy-start.6 = (bf16[3,3,3,128,128]{4,3,2,1,0:T(8,128)(2,1)S(1)}, bf16[3,3,3,128,128]{4,3,2,1,0:T(8,128)(2,1)}, u32[]{:S(2)}) copy-start(bf16[3,3,3,128,128]{4,3,2,1,0:T(8,128)(2,1)} %param.8) | copy-start | bytes 2654212
  1.6 19.6 %collective-permute-start = (bf16[2,1,128,128]{3,2,1,0:T(8,128)(2,1)S(1)}, bf16[2,1,128,128]{3,2,1,0:T(8,128)(2,1)S(1)}, u32[]{:S(2)}, u32[]{:S(2)}) collective-permute-start(bf16[2,1,128,128]{3,2,1,0:T(8,128)(2,1)S(1)} %get-tuple-element.17), channel_id=1, source_target_pairs={{0,1},{1,2},{2,3},{3,4},{4,5},{5,6},{6,7},{7,8},{8,9},{9,10},{10,1... | collective-permute-start | bytes 196616 | tf_op jit(solution)/shard_map/ppermute | solution.py:16
  5.1 16.1 %collective-permute-start.1 = (bf16[2,1,128,128]{3,2,1,0:T(8,128)(2,1)S(1)}, bf16[2,1,128,128]{3,2,1,0:T(8,128)(2,1)S(1)}, u32[]{:S(2)}, u32[]{:S(2)}) collective-permute-start(bf16[2,1,128,128]{3,2,1,0:T(8,128)(2,1)S(1)} %get-tuple-element.18), channel_id=1, source_target_pairs={{1,0},{2,1},{3,2},{4,3},{5,4},{6,5},{7,6},{8,7},{9,8},{10,9},{11,1... | collective-permute-start | bytes 196616 | tf_op jit(solution)/shard_map/ppermute | solution.py:18
  7.2 8.8 %collective-permute-start.5 = (bf16[1,1,64,128]{3,2,1,0:T(8,128)(2,1)S(1)}, bf16[1,1,64,128]{3,2,1,0:T(8,128)(2,1)S(1)}, u32[]{:S(2)}, u32[]{:S(2)}) collective-permute-start(bf16[1,1,64,128]{3,2,1,0:T(8,128)(2,1)S(1)} %slice.442), channel_id=1, source_target_pairs={{1,0},{2,1},{3,2},{4,3},{5,4},{6,5},{7,6},{8,7},{9,8},{10,9},{11,1... | collective-permute-start | bytes 49160 | tf_op jit(solution)/shard_map/ppermute | solution.py:28
  11.6 13.5 %copy-start.8 = (pred[8,18]{0,1:T(8,128)(4,1)S(1)}, pred[8,18]{0,1:T(8,128)(4,1)}, u32[]{:S(2)}) copy-start(pred[8,18]{0,1:T(8,128)(4,1)} %constant.62) | copy-start | bytes 436
  16.0 7.3 %collective-permute-start.6 = (bf16[1,3,64,128]{3,2,1,0:T(8,128)(2,1)S(1)}, bf16[1,3,64,128]{3,2,1,0:T(8,128)(2,1)S(1)}, u32[]{:S(2)}, u32[]{:S(2)}) collective-permute-start(bf16[1,3,64,128]{3,2,1,0:T(8,128)(2,1)S(1)} %pad_maximum_fusion.7), channel_id=1, source_target_pairs={{16,0},{32,16},{48,32},{64,48},{80,64},{96,80},{112,96},{17,1},{33... | collective-permute-start | bytes 147464 | tf_op jit(solution)/shard_map/ppermute | solution.py:28
  21.3 9.7 %collective-permute-start.2 = (bf16[2,6,128,128]{3,2,1,0:T(8,128)(2,1)S(1)}, bf16[2,6,128,128]{3,2,1,0:T(8,128)(2,1)S(1)}, u32[]{:S(2)}, u32[]{:S(2)}) collective-permute-start(bf16[2,6,128,128]{3,2,1,0:T(8,128)(2,1)S(1)} %pad_maximum_fusion.3), channel_id=1, source_target_pairs={{0,16},{16,32},{32,48},{48,64},{64,80},{80,96},{96,112},{1,17},{17... | collective-permute-start | bytes 1179656 | tf_op jit(solution)/shard_map/ppermute | solution.py:28
  35.5 8.0 %collective-permute-start.3 = (bf16[2,1,128,128]{3,2,1,0:T(8,128)(2,1)S(1)}, bf16[2,1,128,128]{3,2,1,0:T(8,128)(2,1)S(1)}, u32[]{:S(2)}, u32[]{:S(2)}) collective-permute-start(bf16[2,1,128,128]{3,2,1,0:T(8,128)(2,1)S(1)} %slice.437), channel_id=1, source_target_pairs={{0,1},{1,2},{2,3},{3,4},{4,5},{5,6},{6,7},{7,8},{8,9},{9,10},{10,1... | collective-permute-start | bytes 196616 | tf_op jit(solution)/shard_map/ppermute | solution.py:28
  43.5 4.9 %copy-start.7 = (bf16[1,1,2,64,128]{4,3,2,1,0:T(8,128)(2,1)S(1)}, bf16[1,1,2,64,128]{4,3,2,1,0:T(8,128)(2,1)}, u32[]{:S(2)}) copy-start(bf16[1,1,2,64,128]{4,3,2,1,0:T(8,128)(2,1)} %param.9) | copy-start | bytes 98308
  44.8 9.0 %collective-permute-start.4 = (bf16[2,5,128,128]{3,2,1,0:T(8,128)(2,1)S(1)}, bf16[2,5,128,128]{3,2,1,0:T(8,128)(2,1)S(1)}, u32[]{:S(2)}, u32[]{:S(2)}) collective-permute-start(bf16[2,5,128,128]{3,2,1,0:T(8,128)(2,1)S(1)} %pad_maximum_fusion.2), channel_id=1, source_target_pairs={{0,16},{16,32},{32,48},{48,64},{64,80},{80,96},{96,112},{1,17},{17... | collective-permute-start | bytes 983048 | tf_op jit(solution)/shard_map/ppermute | solution.py:28
  48.2 8.4 %copy-start.1 = (bf16[1,2,64,1152]{3,2,1,0:T(8,128)(2,1)}, bf16[1,2,64,1152]{3,2,1,0:T(8,128)(2,1)S(1)}, u32[]{:S(2)}) copy-start(bf16[1,2,64,1152]{3,2,1,0:T(8,128)(2,1)S(1)} %constant_dynamic-update-slice_fusion.19) | copy-start | bytes 884740
  56.5 0.7 copy-start.3
  56.8 0.7 copy-start.4
  255.0 7.1 %copy-start.2 = (bf16[1,2,64,1152]{3,2,1,0:T(8,128)(2,1)S(1)}, bf16[1,2,64,1152]{3,2,1,0:T(8,128)(2,1)}, u32[]{:S(2)}) copy-start(bf16[1,2,64,1152]{3,2,1,0:T(8,128)(2,1)} %copy-done.1) | copy-start | bytes 884740
  255.0 7.1 %copy-start.5 = (bf16[1,3,3,128,128]{4,3,2,1,0:T(8,128)(2,1)S(1)}, bf16[1,3,3,128,128]{4,3,2,1,0:T(8,128)(2,1)}, u32[]{:S(2)}) copy-start(bf16[1,3,3,128,128]{4,3,2,1,0:T(8,128)(2,1)} %get-tuple-element.7) | copy-start | bytes 884740
where the time goes:
time: 264 us; the launch traced here: 263 us
  blocking collectives  196 us (74%)
  starting transfers between devices  21.6 us (8%)
  local copies, waits for them, and re-layouts  15.7 us (6%)
  matrix products  12.9 us (5%)
  waiting for transfers between devices  8.16 us (3%)
  other arithmetic  5.58 us (2%)
  between operations  3.58 us (1%)
    psum x1, blocking collectives, body(): lax.psum((first_local, down_local), ('dp', 'tm', 'height'))  196 us
    ppermute x5, starting transfers between devices, shifted(): lax.ppermute(value, axis, [(source, source + steps) for source in range(l...  16.8 us
    ppermute x5, waiting for transfers between devices, shifted(): lax.ppermute(value, axis, [(source, source + steps) for source in range(l...  8.16 us
    dot_general x6, matrix products, conv_layer(): jnp.dot(columns, kernel, preferred_element_type=jnp.float32)  7.65 us
  transfers between devices with their start and end apart: 7, of which 2 were waited for; matrix products, arithmetic and copies ran while one was open for 5% of the time, Pallas kernels for 0%

commit v1 on v0

--- a/solution.py
+++ b/solution.py
@@ -155,7 +155,9 @@
     )
     first_local = weight_grad(input_ext, pre_grad, first_mask, 1, (1, 1))
     share = conv_first.shape[3] // lax.axis_size("dp")
-    summed_first, summed_down = lax.psum((first_local, down_local), ("dp", "tm", "height"))
+    summed_first, summed_down = lax.psum(
+        lax.psum((first_local, down_local), ("tm", "height")), "dp"
+    )
     offset = lax.axis_index("dp") * share
     summed_first = lax.dynamic_slice_in_dim(summed_first, offset, share, 3)
     summed_down = lax.dynamic_slice_in_dim(summed_down, offset, share, 3)

time: 264 us -> 2210 us (8.37)
  the two profiles are of different devices: /device:TPU:32 before, /device:TPU:1 now
where the time goes in v1:
time: 2210 us
  waiting for transfers between devices  1940 us (88%)
  blocking collectives  203 us (9%)
    psum x1, waiting for transfers between devices, body(): lax.psum((first_local, down_local), ('tm', 'height'))  1940 us
    psum x1, blocking collectives, body(): lax.psum(lax.psum((first_local, down_local), ('tm', 'height')), 'dp')  203 us
  transfers between devices with their start and end apart: 8, of which 3 were waited for; matrix products, arithmetic and copies ran while one was open for 1% of the time, Pallas kernels for 0%

profile of v1, /device:TPU:1, one launch (start us, length us, event | category | flops | bytes accessed | tf_op | source)
XLA Modules:
  0.0 2213.9 jit_solution(9726102489325543180)
XLA Ops:
  7.2 0.9 fusion.93
  8.1 4.0 collective-permute-start
  12.2 1.3 collective-permute-start.1
  13.5 0.8 fusion.63
  14.3 1.3 collective-permute-start.5
  15.6 0.8 reduce-window_clone.1
  16.4 0.7 subtract_bitcast_fusion
  17.1 0.2 fusion.68
  17.4 1.3 fusion.91
  18.7 0.6 fusion.94
  19.3 0.6 slice.447
  19.9 0.6 slice.451
  22.4 1.3 collective-permute-start.6
  23.8 4.2 collective-permute-start.2
  28.1 1.3 multiply_bitcast_fusion.1
  29.9 0.3 convolution_select_fusion.2
  30.2 0.3 fusion.4
  30.6 0.1 slice_dynamic-update-slice_fusion.10
  30.7 0.1 slice_dynamic-update-slice_fusion.9
  30.9 0.3 fusion.3
  31.3 0.1 slice_dynamic-update-slice_fusion.8
  31.7 0.1 slice_dynamic-update-slice_fusion.7
  31.9 0.1 slice_dynamic-update-slice_fusion.6
  32.0 0.7 collective-permute-done.2
  33.0 0.1 slice_dynamic-update-slice_fusion.16
  33.1 0.1 slice_dynamic-update-slice_fusion.15
  33.3 0.1 slice_dynamic-update-slice_fusion.14
  33.4 0.1 slice_dynamic-update-slice_fusion.13
  33.6 0.1 slice_dynamic-update-slice_fusion.12
  33.8 0.8 convolution_multiply_fusion.1
  34.7 0.1 slice_dynamic-update-slice_fusion.22
  34.8 0.1 slice_dynamic-update-slice_fusion.21
  35.0 0.1 slice_dynamic-update-slice_fusion.20
  35.1 0.1 slice_dynamic-update-slice_fusion.19
  35.3 0.1 slice_dynamic-update-slice_fusion.18
  35.4 0.8 fusion.1
  36.2 0.9 fusion.10
  37.2 4.6 collective-permute-start.3
  41.8 0.9 fusion.26
  42.7 0.9 fusion.24
  43.6 0.9 fusion.22
  44.4 1.4 pad_maximum_fusion
  46.5 0.1 slice.408
  46.7 0.1 slice.409
  46.8 0.2 slice.410
  47.1 4.8 collective-permute-start.4
  52.2 0.3 convolution_bitcast_fusion
  52.5 3.3 collective-permute-done.4
  56.5 0.1 slice.396
  56.7 0.1 slice.397
  56.8 0.2 slice.398
  57.8 0.1 slice.384
  57.9 0.1 slice.385
  58.1 0.2 slice.386
  58.8 0.3 convolution_bitcast_fusion.1
  59.1 0.3 convolution_bitcast_fusion.2
  59.4 1.4 pad_maximum_fusion.1
  60.9 0.8 convolution_multiply_fusion.5
  61.7 0.9 fusion.6
  62.6 1.5 fusion.8
  64.1 1938.4 %all-reduce.11.cloned.1.call-done = (f32[3,3,3,128,128]{4,3,2,1,0:T(8,128)}, f32[3,3,3,128,128]{4,3,2,1,0:T(8,128)}) async-done(((f32[3,3,3,128,128]{4,3,2,1,0:T(8,128)}, f32[3,3,3,128,128]{4,3,2,1,0:T(8,128)}), (f32[3,3,3,128,128]{4,3,2,1,0:T(8,128)}, f32[3,3,3,128,128]{4,3,2,1,0:T(8,128)})) %all-reduce.11.cloned.1.call-update) | async-done | bytes 3538960 | tf_op jit(solution)/shard_map/psum | solution.py:159
  2002.5 203.2 %all-reduce.12 = (bf16[3,3,3,128,128]{4,3,2,1,0:T(8,128)(2,1)S(1)}, bf16[3,3,3,128,128]{4,3,2,1,0:T(8,128)(2,1)S(1)}) all-reduce(f32[3,3,3,128,128]{4,3,2,1,0:T(8,128)} %get-tuple-element.5, f32[3,3,3,128,128]{4,3,2,1,0:T(8,128)} %get-tuple-element.6), channel_id=1, replica_groups=mesh['dp'=4,'tm'=8,'height'=16] {'dp'}, use_global_device_ids=true, to_apply=%region_4.5 | all-reduce | flops 884736 | bytes 5308416 | tf_op jit(solution)/shard_map/psum | solution.py:158
  2205.7 0.7 dynamic-slice_convert_fusion
  2206.4 0.7 dynamic-slice_convert_fusion.1
  (115 shorter events, 4.4 us)
Async XLA Ops:
  7.2 16.6 copy-start
  7.2 1995.3 %all-reduce.11.cloned.1.call-start = ((), (), s32[]{:S(2)}) async-start(), calls=%async_computation | async-start | bytes 7077888 | tf_op jit(solution)/shard_map/psum | solution.py:159
  8.1 15.6 collective-permute-start
  12.2 11.6 collective-permute-start.1
  14.3 8.2 collective-permute-start.5
  17.4 12.4 copy-start.1
  17.4 12.4 copy-start.3
  22.4 5.7 collective-permute-start.6
  23.8 8.9 collective-permute-start.2
  37.2 8.6 collective-permute-start.3
  45.8 6.4 copy-start.2
  47.1 8.6 collective-permute-start.4
Sparse Core Ops, SparseCore 0:
  60.9 1941.4 all-reduce.10
